TPU v7x, 256 devices: a whole 4x4x8 slice. The times are simulated.
256 devices in a mesh: expert: 16 (over x, y), dp: 16 (over z, core).
Axes of the slice: x: 4, y: 4, z: 8, core: 2. Of those that a mesh axis runs over, the one named last changes fastest.
Arguments:
- tokens: bfloat16 [4096, 4096], P(('expert', 'dp')), may hold values from -6 to 6
- grad_out: bfloat16 [4096, 4096], P(('expert', 'dp')), may hold values from -6 to 6
- gate_values: bfloat16 [4096, 2], P(('expert', 'dp')), may hold values from 0.099609375 to 1
- routes: int32 [4096, 2], P(('expert', 'dp')), may hold values from 0 to 31, all different within a row; in each aligned block of 16 rows (0 to 15, 16 to 31, ...) at most 2 rows name the same one
- gate_weight: bfloat16 [32, 1536, 4096], P('expert', 'dp'), may hold values from -0.09375 to 0.09375
- up_weight: bfloat16 [32, 1536, 4096], P('expert', 'dp'), may hold values from -0.09375 to 0.09375
- down_weight: bfloat16 [32, 1536, 4096], P('expert', 'dp'), may hold values from -0.15625 to 0.15625
Outputs:
- grad_tokens: bfloat16 [4096, 4096], P(('expert', 'dp'))
- grad_gates: float32 [4096, 2], P(('expert', 'dp'))
- grad_gate_weight: bfloat16 [32, 1536, 4096], P('expert', 'dp')
- grad_up_weight: bfloat16 [32, 1536, 4096], P('expert', 'dp')
- grad_down_weight: bfloat16 [32, 1536, 4096], P('expert', 'dp')
Inputs may be any that keep to these rules, and one draw needn't show every extreme that they name: `routes`: each row names 2 different experts. In each aligned block of 16 rows (the rows of one device) no expert is named by more than 2 rows, a bound that some block reaches.
All inputs are finite; a program needn't handle non-finite values.
Results may differ from a plain program's by a relative error of at most 0.019.
Values may be sent and summed in bfloat16 or wider, within the bound.
No kernel may reach another device: no remote copies, remote signals or barrier semaphores. Data moves between devices by JAX's collectives and lax.ppermute only.
A program may use at most 128 MiB of HBM per device.

v0:
```python
import jax
import jax.numpy as jnp
from jax import lax
from jax.sharding import PartitionSpec as P


def per_device(tokens, grad_out, gate_values, routes, gate_weight, up_weight, down_weight):
    tok_rows, model_width = tokens.shape
    chosen = routes.shape[1]
    local_experts = gate_weight.shape[0]
    groups = lax.axis_size("expert")
    replicas = lax.axis_size("dp")
    experts_all = local_experts * groups
    capacity = 2 * tok_rows * chosen // experts_all
    slot_count = experts_all * capacity
    flat_routes = routes.reshape(-1)
    onehot = (flat_routes[:, None] == jnp.arange(experts_all, dtype=jnp.int32)[None, :]).astype(
        jnp.int32
    )
    earlier = jnp.cumsum(onehot, axis=0) - onehot
    slot_rank = jnp.sum(earlier * onehot, axis=1)
    owner_col = flat_routes // local_experts
    local_id = flat_routes % local_experts
    slot_index = (local_id * groups + owner_col) * capacity + slot_rank
    placing = (jnp.arange(slot_count, dtype=jnp.int32)[:, None] == slot_index[None, :]).astype(
        jnp.float32
    )
    token_map = jnp.sum(placing.reshape(slot_count, tok_rows, chosen), axis=2).astype(jnp.bfloat16)
    slot_gates = jnp.dot(
        placing.astype(jnp.bfloat16), gate_values.reshape(-1), preferred_element_type=jnp.float32
    ).astype(jnp.bfloat16)
    x_slots = jnp.dot(token_map, tokens, preferred_element_type=jnp.float32).astype(jnp.bfloat16)
    dy_slots = jnp.dot(token_map, grad_out, preferred_element_type=jnp.float32).astype(jnp.bfloat16)
    block_shape = (local_experts, groups, capacity, model_width)
    arrived = (
        lax.all_to_all(
            x_slots.reshape(block_shape), "expert", split_axis=1, concat_axis=1, tiled=True
        ),
        lax.all_to_all(
            dy_slots.reshape(block_shape), "expert", split_axis=1, concat_axis=1, tiled=True
        ),
        lax.all_to_all(
            slot_gates.reshape(block_shape[:3]), "expert", split_axis=1, concat_axis=1, tiled=True
        ),
    )
    x_rows, dy_rows, gate_rows = (
        lax.all_gather(arrived[0], "dp", axis=2, tiled=True),
        lax.all_gather(arrived[1], "dp", axis=2, tiled=True),
        lax.all_gather(arrived[2], "dp", axis=2, tiled=True),
    )
    row_total = groups * replicas * capacity
    inputs = x_rows.reshape(local_experts, row_total, model_width)
    upstream = dy_rows.reshape(local_experts, row_total, model_width)
    weighting = gate_rows.reshape(local_experts, row_total).astype(jnp.float32)[..., None]
    gate_pre = jnp.einsum("lrd,lhd->lrh", inputs, gate_weight, preferred_element_type=jnp.float32)
    up_pre = jnp.einsum("lrd,lhd->lrh", inputs, up_weight, preferred_element_type=jnp.float32)
    back_hidden = jnp.einsum(
        "lrd,lhd->lrh", upstream, down_weight, preferred_element_type=jnp.float32
    )
    sigmoid_gate = jax.nn.sigmoid(gate_pre)
    activated = gate_pre * sigmoid_gate
    hidden = activated * up_pre
    gate_part = jnp.sum(back_hidden * hidden, axis=2)
    scaled = weighting * back_hidden
    grad_gate_pre = (
        scaled * up_pre * sigmoid_gate * (1.0 + gate_pre * (1.0 - sigmoid_gate))
    ).astype(jnp.bfloat16)
    grad_up_pre = (scaled * activated).astype(jnp.bfloat16)
    weighted_hidden = (weighting * hidden).astype(jnp.bfloat16)
    input_part = jnp.einsum(
        "lrh,lhd->lrd", grad_gate_pre, gate_weight, preferred_element_type=jnp.float32
    )
    input_part = input_part + jnp.einsum(
        "lrh,lhd->lrd", grad_up_pre, up_weight, preferred_element_type=jnp.float32
    )
    grad_gate_weight = jnp.einsum(
        "lrh,lrd->lhd", grad_gate_pre, inputs, preferred_element_type=jnp.float32
    ).astype(jnp.bfloat16)
    grad_up_weight = jnp.einsum(
        "lrh,lrd->lhd", grad_up_pre, inputs, preferred_element_type=jnp.float32
    ).astype(jnp.bfloat16)
    grad_down_weight = jnp.einsum(
        "lrh,lrd->lhd", weighted_hidden, upstream, preferred_element_type=jnp.float32
    ).astype(jnp.bfloat16)
    part_shape = (local_experts, groups, replicas * capacity, model_width)
    summed = lax.psum_scatter(
        input_part.reshape(part_shape).astype(jnp.bfloat16), "dp", scatter_dimension=2, tiled=True
    )
    returned = lax.all_to_all(summed, "expert", split_axis=1, concat_axis=1, tiled=True)
    returned = returned.reshape(slot_count, model_width)
    grad_tokens = lax.dot_general(
        token_map, returned, (((0,), (0,)), ((), ())), preferred_element_type=jnp.float32
    ).astype(jnp.bfloat16)
    gate_share = gate_part.reshape(local_experts, groups, replicas * capacity)
    gate_total = lax.psum(gate_share, "dp")
    own_gates = lax.dynamic_slice_in_dim(gate_total, lax.axis_index("dp") * capacity, capacity, 2)
    gate_back = lax.all_to_all(
        own_gates, "expert", split_axis=1, concat_axis=1, tiled=True
    ).reshape(slot_count)
    grad_gates = jnp.dot(gate_back, placing, precision=lax.Precision.HIGHEST).reshape(
        tok_rows, chosen
    )
    return (grad_tokens, grad_gates, grad_gate_weight, grad_up_weight, grad_down_weight)


def solution(mesh):
    return jax.shard_map(
        per_device,
        mesh=mesh,
        in_specs=(
            P(("expert", "dp"), None),
            P(("expert", "dp"), None),
            P(("expert", "dp"), None),
            P(("expert", "dp"), None),
            P("expert", "dp", None),
            P("expert", "dp", None),
            P("expert", "dp", None),
        ),
        out_specs=(
            P(("expert", "dp"), None),
            P(("expert", "dp"), None),
            P("expert", "dp", None),
            P("expert", "dp", None),
            P("expert", "dp", None),
        ),
        check_vma=False,
    )
```

profile of v0, /device:TPU:8, one launch (start us, length us, event | category | flops | bytes accessed | tf_op | source)
XLA Modules:
  0.0 287.3 jit_solution(16650401668262213078)
XLA Ops:
  7.2 0.9 copy.82
  8.8 1.2 convolution_convert_fusion.3
  10.4 0.5 copy.95
  10.8 17.3 %all_to_all.25 = bf16[2,16,2,4096]{3,2,0,1:T(2,128)(2,1)S(1)} all-to-all(bf16[2,16,2,4096]{3,2,0,1:T(2,128)(2,1)S(1)} %copy.95), channel_id=1, replica_groups=mesh['expert'=16,'dp'=16] {'expert'}, dimensions={1} | all-to-all | bytes 1048576 | tf_op jit(solution)/shard_map/all_to_all | solution.py:36
  28.2 1.1 copy.96
  29.3 1.2 convolution_convert_fusion.4
  31.4 13.7 %all_to_all.26 = bf16[2,16,2,4096]{3,2,0,1:T(2,128)(2,1)S(1)} all-to-all(bf16[2,16,2,4096]{3,2,0,1:T(2,128)(2,1)S(1)} %copy.92), channel_id=1, replica_groups=mesh['expert'=16,'dp'=16] {'expert'}, dimensions={1} | all-to-all | bytes 1048576 | tf_op jit(solution)/shard_map/all_to_all | solution.py:39
  45.0 1.1 copy.93
  46.7 10.8 %all_to_all.27 = bf16[2,16,2]{2,0,1:T(2,128)(2,1)S(1)} all-to-all(bf16[2,16,2]{2,0,1:T(2,128)(2,1)S(1)} %copy.89), channel_id=1, replica_groups=mesh['expert'=16,'dp'=16] {'expert'}, dimensions={1} | all-to-all | bytes 256 | tf_op jit(solution)/shard_map/all_to_all | solution.py:42
  57.6 20.6 %all_gather.9 = bf16[2,16,32]{1,0,2:T(2,128)(2,1)S(1)} all-gather(bf16[2,16,2]{1,0,2:T(2,128)(2,1)S(1)} %copy.90), channel_id=1, replica_groups=mesh['expert'=16,'dp'=16] {'dp'}, dimensions={2}, use_global_device_ids=true | all-gather | bytes 2176 | tf_op jit(solution)/shard_map/all_gather | solution.py:49
  78.4 7.3 %all-gather.5.cloned.1.call-done = bf16[2,16,32,4096]{3,1,0,2:T(8,128)(2,1)} async-done(((bf16[2,16,2,4096]{3,1,0,2:T(8,128)(2,1)}), bf16[2,16,32,4096]{3,1,0,2:T(8,128)(2,1)}) %all-gather.5.cloned.1.call-update) | async-done | bytes 8388624 | tf_op jit(solution)/shard_map/all_gather | solution.py:47
  85.7 11.2 %copy.97 = bf16[2,16,32,4096]{3,2,1,0:T(8,128)(2,1)} copy(bf16[2,16,32,4096]{3,1,0,2:T(8,128)(2,1)} %all-gather.5.cloned.1.call-done) | data formatting | bytes 16777216 | tf_op jit(solution)/shard_map/all_gather | solution.py:47
  96.9 6.6 %fusion.23 = f32[2,512,96]{1,2,0:T(8,128)S(1)} fusion(bf16[2,512,4096]{2,1,0:T(8,128)(2,1)} %bitcast.33, bf16[2,96,4096]{2,1,0:T(8,128)(2,1)S(1)} %copy-done), kind=kOutput, calls=%fused_computation.55 | convolution fusion | flops 805306368 | bytes 10354688 | tf_op jit(solution)/shard_map/lrd,lhd->lrh/dot_general | solution.py:55
  103.5 2.7 fusion.22
  106.2 36.3 %all-gather.3.cloned.1.call-done = bf16[2,16,32,4096]{3,1,0,2:T(8,128)(2,1)} async-done(((bf16[2,16,2,4096]{3,1,0,2:T(8,128)(2,1)}), bf16[2,16,32,4096]{3,1,0,2:T(8,128)(2,1)}) %all-gather.3.cloned.1.call-update) | async-done | bytes 8388624 | tf_op jit(solution)/shard_map/all_gather | solution.py:48
  142.5 11.5 %copy.94 = bf16[2,16,32,4096]{3,2,1,0:T(8,128)(2,1)} copy(bf16[2,16,32,4096]{3,1,0,2:T(8,128)(2,1)} %all-gather.3.cloned.1.call-done) | data formatting | bytes 16777216 | tf_op jit(solution)/shard_map/all_gather | solution.py:48
  154.0 6.2 %multiply_reduce_fusion = (f32[2,512]{1,0:T(2,128)S(1)}, bf16[2,512,96]{1,2,0:T(8,128)(2,1)S(1)}, bf16[2,512,96]{1,2,0:T(8,128)(2,1)S(1)}) fusion(f32[2,512,96]{1,2,0:T(8,128)S(1)} %fusion.22, f32[2,512,96]{1,2,0:T(8,128)S(1)} %fusion.23, f32[2,512]{1,0:T(2,128)S(1)} %reshape.148, bf16[2,512,4096]{2,1,0:T(8,128)(2,1)} %bitcast.37, ...), kind=kOutput, calls=%fused_computation.10 | convolution fusion | flops 806976512 | bytes 11149312 | tf_op jit(solution)/shard_map/lrd,lhd->lrh/dot_general | solution.py:57
  160.2 8.1 %fusion.24 = f32[2,512,4096]{2,1,0:T(8,128)} fusion(bf16[2,512,96]{1,2,0:T(8,128)(2,1)S(1)} %get-tuple-element.6, bf16[2,96,4096]{2,1,0:T(8,128)(2,1)S(1)} %copy-done), kind=kOutput, calls=%fused_computation.56 | convolution fusion | flops 805306368 | bytes 18546688 | tf_op jit(solution)/shard_map/lrh,lhd->lrd/dot_general | solution.py:70
  168.3 11.4 %add_convert_fusion = bf16[2,512,4096]{2,1,0:T(8,128)(2,1)} fusion(f32[2,512,4096]{2,1,0:T(8,128)} %fusion.24, bf16[2,512,96]{1,2,0:T(8,128)(2,1)S(1)} %get-tuple-element.7, bf16[2,96,4096]{2,1,0:T(8,128)(2,1)S(1)} %copy-done.4), kind=kOutput, calls=%fused_computation | convolution fusion | flops 813694976 | bytes 26935296 | tf_op jit(solution)/shard_map/lrh,lhd->lrd/dot_general | solution.py:73
  179.8 11.4 %copy.98 = bf16[2,16,32,4096]{3,1,0,2:T(8,128)(2,1)} copy(bf16[2,16,32,4096]{3,2,1,0:T(8,128)(2,1)} %bitcast.39) | data formatting | bytes 16777216 | tf_op jit(solution)/shard_map/convert_element_type | solution.py:87
  191.4 46.9 %psum.7 = f32[2,16,32]{2,1,0:T(8,128)S(1)} all-reduce(f32[2,16,32]{2,1,0:T(8,128)S(1)} %reshape.146), channel_id=1, replica_groups=mesh['expert'=16,'dp'=16] {'dp'}, use_global_device_ids=true, to_apply=%region_5.6 | all-reduce | flops 1024 | bytes 8192 | tf_op jit(solution)/shard_map/psum | solution.py:95
  238.4 0.6 copy.101
  239.0 7.3 %all-to-all-start.4 = ((f32[2,16,2]{2,0,1:T(2,128)}), f32[2,16,2]{2,0,1:T(2,128)S(1)}, u32[]{:S(2)}, u32[]{:S(2)}) async-start(f32[2,16,2]{2,0,1:T(2,128)} %copy.101), calls=%async_computation.5 | async-start | bytes 32768 | tf_op jit(solution)/shard_map/all_to_all | solution.py:97
  246.3 6.2 %convolution_convert_fusion = bf16[2,96,4096]{2,1,0:T(8,128)(2,1)} fusion(bf16[2,512,4096]{2,1,0:T(8,128)(2,1)} %bitcast.38, f32[2,512]{1,0:T(2,128)S(1)} %reshape.148, f32[2,512,96]{1,2,0:T(8,128)S(1)} %fusion.22, f32[2,512,96]{1,2,0:T(8,128)S(1)} %fusion.23), kind=kOutput, calls=%fused_computation.1 | convolution fusion | flops 806780928 | bytes 10752000 | tf_op jit(solution)/shard_map/lrh,lrd->lhd/dot_general | solution.py:82
  252.5 6.2 %convolution_convert_fusion.2 = bf16[2,96,4096]{2,1,0:T(8,128)(2,1)} fusion(bf16[2,512,96]{1,2,0:T(8,128)(2,1)S(1)} %get-tuple-element.6, bf16[2,512,4096]{2,1,0:T(8,128)(2,1)} %bitcast.34), kind=kOutput, calls=%fused_computation.3 | convolution fusion | flops 806092800 | bytes 10158080 | tf_op jit(solution)/shard_map/lrh,lrd->lhd/dot_general | solution.py:76
  258.6 2.4 reduce-scatter.2.cloned.1.call-done
  261.0 2.4 copy.99
  263.4 7.1 %all-to-all-start.3 = ((bf16[2,16,2,4096]{3,2,0,1:T(2,128)(2,1)}), bf16[2,16,2,4096]{3,2,0,1:T(2,128)(2,1)S(1)}, u32[]{:S(2)}, u32[]{:S(2)}) async-start(bf16[2,16,2,4096]{3,2,0,1:T(2,128)(2,1)} %copy.99), calls=%async_computation.4 | async-start | bytes 1048576 | tf_op jit(solution)/shard_map/all_to_all | solution.py:89
  270.5 6.1 %convolution_convert_fusion.1 = bf16[2,96,4096]{2,1,0:T(8,128)(2,1)} fusion(bf16[2,512,96]{1,2,0:T(8,128)(2,1)S(1)} %get-tuple-element.7, bf16[2,512,4096]{2,1,0:T(8,128)(2,1)} %bitcast.35), kind=kOutput, calls=%fused_computation.2 | convolution fusion | flops 806092800 | bytes 10158080 | tf_op jit(solution)/shard_map/lrh,lrd->lhd/dot_general | solution.py:79
  276.7 0.8 fusion.6
  277.5 1.8 all-to-all-done.3
  279.9 0.9 convolution_convert_fusion.5
  (49 shorter events, 3.8 us)
Async XLA Ops:
  7.2 89.7 %copy-start = (bf16[2,96,4096]{2,1,0:T(8,128)(2,1)S(1)}, bf16[2,96,4096]{2,1,0:T(8,128)(2,1)}, u32[]{:S(2)}) copy-start(bf16[2,96,4096]{2,1,0:T(8,128)(2,1)} %param.11) | copy-start | bytes 4718596
  7.2 39.0 %copy-start.6 = (bf16[16,2]{0,1:T(2,128)(2,1)S(1)}, bf16[16,2]{0,1:T(2,128)(2,1)}, u32[]{:S(2)}) copy-start(bf16[16,2]{0,1:T(2,128)(2,1)} %param.9) | copy-start | bytes 196
  7.2 78.5 %all-gather.5.cloned.1.call-start = ((), (), s32[]{:S(2)}) async-start(), calls=%async_computation.7 | async-start | bytes 8912896 | tf_op jit(solution)/shard_map/all_gather | solution.py:47
  29.3 113.3 %all-gather.3.cloned.1.call-start = ((), (), s32[]{:S(2)}) async-start(), calls=%async_computation.6 | async-start | bytes 8912896 | tf_op jit(solution)/shard_map/all_gather | solution.py:48
  46.1 214.9 %reduce-scatter.2.cloned.1.call-start = ((), (), s32[]{:S(2)}) async-start(), calls=%async_computation.8 | async-start | bytes 8912896 | tf_op jit(solution)/shard_map/reduce_scatter | solution.py:86
  96.9 6.6 %copy-start.2 = (bf16[2,16,32,4096]{3,2,1,0:T(8,128)(2,1)S(1)}, bf16[2,16,32,4096]{3,2,1,0:T(8,128)(2,1)}, u32[]{:S(2)}) copy-start(bf16[2,16,32,4096]{3,2,1,0:T(8,128)(2,1)} %copy.97) | copy-start | bytes 25165828
  96.9 6.6 %copy-start.3 = (bf16[2,96,4096]{2,1,0:T(8,128)(2,1)S(1)}, bf16[2,96,4096]{2,1,0:T(8,128)(2,1)}, u32[]{:S(2)}) copy-start(bf16[2,96,4096]{2,1,0:T(8,128)(2,1)} %param.12) | copy-start | bytes 4718596
  142.5 11.5 %copy-start.5 = (bf16[2,96,4096]{2,1,0:T(8,128)(2,1)S(1)}, bf16[2,96,4096]{2,1,0:T(8,128)(2,1)}, u32[]{:S(2)}) copy-start(bf16[2,96,4096]{2,1,0:T(8,128)(2,1)} %param.13) | copy-start | bytes 4718596
  160.2 8.1 %copy-start.4 = (bf16[2,96,4096]{2,1,0:T(8,128)(2,1)S(1)}, bf16[2,96,4096]{2,1,0:T(8,128)(2,1)}, u32[]{:S(2)}) copy-start(bf16[2,96,4096]{2,1,0:T(8,128)(2,1)} %param.12) | copy-start | bytes 4718596
  239.0 24.4 %all-to-all-start.4 = ((f32[2,16,2]{2,0,1:T(2,128)}), f32[2,16,2]{2,0,1:T(2,128)S(1)}, u32[]{:S(2)}, u32[]{:S(2)}) async-start(f32[2,16,2]{2,0,1:T(2,128)} %copy.101), calls=%async_computation.5 | async-start | bytes 32768 | tf_op jit(solution)/shard_map/all_to_all | solution.py:97
  263.4 15.8 %all-to-all-start.3 = ((bf16[2,16,2,4096]{3,2,0,1:T(2,128)(2,1)}), bf16[2,16,2,4096]{3,2,0,1:T(2,128)(2,1)S(1)}, u32[]{:S(2)}, u32[]{:S(2)}) async-start(bf16[2,16,2,4096]{3,2,0,1:T(2,128)(2,1)} %copy.99), calls=%async_computation.4 | async-start | bytes 1048576 | tf_op jit(solution)/shard_map/all_to_all | solution.py:89
  270.5 10.2 %copy-start.1 = (bf16[2,96,4096]{2,1,0:T(8,128)(2,1)S(1)}, bf16[2,96,4096]{2,1,0:T(8,128)(2,1)}, u32[]{:S(2)}) copy-start(bf16[2,96,4096]{2,1,0:T(8,128)(2,1)} %param.11) | copy-start | bytes 4718596
Sparse Core Ops, SparseCore 0:
  29.4 56.2 all-gather.4
  88.1 54.3 all-gather.2
  191.4 69.5 reduce-scatter.1
where the time goes:
time: 288 us; the launch traced here: 287 us
  blocking collectives  109 us (38%)
  matrix products  57.6 us (20%)
  waiting for transfers between devices  47.8 us (17%)
  local copies, waits for them, and re-layouts  43.6 us (15%)
  starting transfers between devices  14.5 us (5%)
  between operations  13.9 us (5%)
    psum x1, blocking collectives, per_device(): gate_total = lax.psum(gate_share, 'dp')  46.9 us
    all_gather x1, waiting for transfers between devices, per_device(): lax.all_gather(arrived[1], 'dp', axis=2, tiled=True)  36.3 us
    all_gather x1, blocking collectives, per_device(): lax.all_gather(arrived[2], 'dp', axis=2, tiled=True)  20.6 us
    all_to_all x1, blocking collectives, per_device(): lax.all_to_all(x_slots.reshape(block_shape), 'expert', split_axis=1, conc...  17.3 us
    all_to_all x1, blocking collectives, per_device(): lax.all_to_all(dy_slots.reshape(block_shape), 'expert', split_axis=1, con...  13.7 us
    all_gather x1, local copies, waits for them, and re-layouts, per_device(): lax.all_gather(arrived[1], 'dp', axis=2, tiled=True)  11.5 us
    convert_element_type x1, local copies, waits for them, and re-layouts, per_device(): input_part.reshape(part_shape).astype(jnp.bfloat16)  11.4 us
    dot_general x1, matrix products, per_device(): jnp.einsum('lrh,lhd->lrd', grad_up_pre, up_weight, preferred_element_type...  11.4 us
  transfers between devices with their start and end apart: 5, of which 4 were waited for; matrix products, arithmetic and copies ran while one was open for 16% of the time, Pallas kernels for 0%

commit v1 on v0

--- a/solution.py
+++ b/solution.py
@@ -2,6 +2,7 @@
 import jax.numpy as jnp
 from jax import lax
 from jax.sharding import PartitionSpec as P
+from jax.lax import all_to_all, axis_size
 
 
 def per_device(tokens, grad_out, gate_values, routes, gate_weight, up_weight, down_weight):
@@ -44,7 +45,7 @@
         ),
     )
     x_rows, dy_rows, gate_rows = (
-        lax.all_gather(arrived[0], "dp", axis=2, tiled=True),
+        jnp.concatenate(all_to_all(jnp.stack([arrived[0]] * axis_size("dp")), "dp", 0, 0), axis=2),
         lax.all_gather(arrived[1], "dp", axis=2, tiled=True),
         lax.all_gather(arrived[2], "dp", axis=2, tiled=True),
     )

time: 288 us -> 479 us (1.66)
  blocking collectives: 109 us -> 279 us
  waiting for transfers between devices: 47.8 us -> 23.7 us
  starting transfers between devices: 14.5 us -> 37.8 us
  local copies, waits for them, and re-layouts: 43.6 us -> 65.4 us
    all_gather x1, blocking collectives: 20.6 us -> 232 us  [per_device(): lax.all_gather(arrived[2], 'dp', axis=2, tiled=True)]
    all_to_all x3 -> x0, blocking collectives: 41.8 us -> none  [the longest x1 17.3 us: per_device(): lax.all_to_all(x_slots.reshape(block_shape), 'expert', split_axis=1, conc...]
    all_gather x1, waiting for transfers between devices: 36.3 us -> 0.02 us  [per_device(): lax.all_gather(arrived[1], 'dp', axis=2, tiled=True)]
    all_to_all x0 -> x4, starting transfers between devices: none -> 25.7 us  [the longest x1 8.62 us: per_device(): all_to_all(jnp.stack([arrived[0]] * axis_size('dp')), 'dp', 0, 0)]
    another operation x0 -> x2, local copies, waits for them, and re-layouts: none -> 21.7 us  [the longest x1 13.1 us: per_device(): inputs = x_rows.reshape(local_experts, row_total, model_width)]
    all_to_all x0 -> x4, waiting for transfers between devices: none -> 17.6 us  [the longest x1 8.37 us: per_device(): lax.all_to_all(dy_slots.reshape(block_shape), 'expert', split_axis=1, con...]
    all_gather x1 -> x0, local copies, waits for them, and re-layouts: 11.2 us -> none  [per_device(): lax.all_gather(arrived[0], 'dp', axis=2, tiled=True)]
    reshape x0 -> x1, local copies, waits for them, and re-layouts: none -> 9.45 us  [per_device(): jnp.concatenate(all_to_all(jnp.stack([arrived[0]] * axis_size('dp')), 'dp...]
  transfers between devices with their start and end apart: 5 -> 8, of which waited for: 4 -> 5; matrix products, arithmetic and copies ran while one was open for 16% -> 13% of each run, Pallas kernels for 0% -> 0%
where the time goes in v1:
time: 479 us; the launch traced here: 478 us
  blocking collectives  279 us (58%)
  local copies, waits for them, and re-layouts  65.4 us (14%)
  matrix products  57.5 us (12%)
  starting transfers between devices  37.8 us (8%)
  waiting for transfers between devices  23.7 us (5%)
  between operations  14.2 us (3%)
    all_gather x1, blocking collectives, per_device(): lax.all_gather(arrived[2], 'dp', axis=2, tiled=True)  232 us
    psum x1, blocking collectives, per_device(): gate_total = lax.psum(gate_share, 'dp')  46.2 us
    another operation x1, local copies, waits for them, and re-layouts, per_device(): inputs = x_rows.reshape(local_experts, row_total, model_width)  13.1 us
    dot_general x1, matrix products, per_device(): jnp.einsum('lrh,lhd->lrd', grad_up_pre, up_weight, preferred_element_type...  11.4 us
    all_gather x1, local copies, waits for them, and re-layouts, per_device(): lax.all_gather(arrived[1], 'dp', axis=2, tiled=True)  11.3 us
    convert_element_type x1, local copies, waits for them, and re-layouts, per_device(): input_part.reshape(part_shape).astype(jnp.bfloat16)  11.2 us
  transfers between devices with their start and end apart: 8, of which 5 were waited for; matrix products, arithmetic and copies ran while one was open for 13% of the time, Pallas kernels for 0%

profile of v1, /device:TPU:8, one launch (start us, length us, event | category | flops | bytes accessed | tf_op | source)
XLA Modules:
  0.0 477.8 jit_solution(17846363597377457881)
XLA Ops:
  10.2 7.4 %all-to-all-start = ((bf16[2,16,2]{2,0,1:T(2,128)(2,1)}), bf16[2,16,2]{2,0,1:T(2,128)(2,1)S(1)}, u32[]{:S(2)}, u32[]{:S(2)}) async-start(bf16[2,16,2]{2,0,1:T(2,128)(2,1)} %copy.89), calls=%async_computation | async-start | bytes 16384 | tf_op jit(solution)/shard_map/all_to_all | solution.py:43
  17.9 1.2 convolution_convert_fusion.3
  19.4 1.3 copy.95
  20.7 3.0 all-to-all-done
  23.7 4.8 %all-to-all-start.2 = ((bf16[2,16,2,4096]{3,2,0,1:T(2,128)(2,1)}), bf16[2,16,2,4096]{3,2,0,1:T(2,128)(2,1)S(1)}, u32[]{:S(2)}, u32[]{:S(2)}) async-start(bf16[2,16,2,4096]{3,2,0,1:T(2,128)(2,1)} %copy.95), calls=%async_computation.2 | async-start | bytes 1048576 | tf_op jit(solution)/shard_map/all_to_all | solution.py:37
  28.6 1.2 convolution_convert_fusion.4
  30.1 1.3 copy.92
  31.4 6.2 %all-to-all-done.2 = bf16[2,16,2,4096]{3,2,0,1:T(2,128)(2,1)S(1)} async-done(((bf16[2,16,2,4096]{3,2,0,1:T(2,128)(2,1)}), bf16[2,16,2,4096]{3,2,0,1:T(2,128)(2,1)S(1)}, u32[]{:S(2)}, u32[]{:S(2)}) %all-to-all-start.2) | async-done | bytes 524320 | tf_op jit(solution)/shard_map/all_to_all | solution.py:37
  37.6 4.8 %all-to-all-start.1 = ((bf16[2,16,2,4096]{3,2,0,1:T(2,128)(2,1)}), bf16[2,16,2,4096]{3,2,0,1:T(2,128)(2,1)S(1)}, u32[]{:S(2)}, u32[]{:S(2)}) async-start(bf16[2,16,2,4096]{3,2,0,1:T(2,128)(2,1)} %copy.92), calls=%async_computation.1 | async-start | bytes 1048576 | tf_op jit(solution)/shard_map/all_to_all | solution.py:40
  42.9 8.4 %all-to-all-done.1 = bf16[2,16,2,4096]{3,2,0,1:T(2,128)(2,1)S(1)} async-done(((bf16[2,16,2,4096]{3,2,0,1:T(2,128)(2,1)}), bf16[2,16,2,4096]{3,2,0,1:T(2,128)(2,1)S(1)}, u32[]{:S(2)}, u32[]{:S(2)}) %all-to-all-start.1) | async-done | bytes 524320 | tf_op jit(solution)/shard_map/all_to_all | solution.py:40
  51.3 8.6 %stack.2 = bf16[16,2,16,2,4096]{4,3,2,1,0:T(2,128)(2,1)} broadcast(bf16[2,16,2,4096]{3,2,1,0:T(2,128)(2,1)S(1)} %copy.96), dimensions={1,2,3,4} | broadcast | bytes 8912896 | tf_op jit(solution)/shard_map/stack | solution.py:48
  59.8 8.6 %all-to-all-start.3 = ((bf16[16,2,16,2,4096]{4,3,2,1,0:T(2,128)(2,1)}), bf16[16,2,16,2,4096]{4,3,2,1,0:T(2,128)(2,1)}, u32[]{:S(2)}, u32[]{:S(2)}) async-start(bf16[16,2,16,2,4096]{4,3,2,1,0:T(2,128)(2,1)} %stack.2), calls=%async_computation.3 | async-start | bytes 16777216 | tf_op jit(solution)/shard_map/all_to_all | solution.py:48
  68.5 1.1 copy.93
  69.8 232.4 %all_gather.6 = bf16[2,16,32]{1,0,2:T(2,128)(2,1)S(1)} all-gather(bf16[2,16,2]{1,0,2:T(2,128)(2,1)S(1)} %copy.90), channel_id=1, replica_groups=mesh['expert'=16,'dp'=16] {'dp'}, dimensions={2}, use_global_device_ids=true | all-gather | bytes 2176 | tf_op jit(solution)/shard_map/all_gather | solution.py:50
  302.3 9.4 %copy.97 = bf16[2,16,16,2,4096]{4,3,2,1,0:T(2,128)(2,1)} copy(bf16[2,16,16,2,4096]{4,3,1,0,2:T(2,128)(2,1)} %bitcast.2) | data formatting | bytes 16777216 | tf_op jit(solution)/shard_map/reshape | solution.py:48
  311.8 13.1 %reshape_reshape.3 = bf16[2,512,4096]{2,1,0:T(8,128)(2,1)} reshape(bf16[2,16,16,2,4096]{4,3,2,1,0:T(2,128)(2,1)} %copy.97) | data formatting | bytes 16777216 | tf_op jit(solution)/shard_map/reshape;reshape | solution.py:53
  324.9 6.2 %fusion.23 = f32[2,512,96]{1,2,0:T(8,128)S(1)} fusion(bf16[2,512,4096]{2,1,0:T(8,128)(2,1)} %reshape_reshape.3, bf16[2,96,4096]{2,1,0:T(8,128)(2,1)S(1)} %copy-done), kind=kOutput, calls=%fused_computation.55 | convolution fusion | flops 805306368 | bytes 10354688 | tf_op jit(solution)/shard_map/lrd,lhd->lrh/dot_general | solution.py:56
  331.2 2.7 fusion.22
  333.9 11.3 %copy.94 = bf16[2,16,32,4096]{3,2,1,0:T(8,128)(2,1)} copy(bf16[2,16,32,4096]{3,1,0,2:T(8,128)(2,1)} %all-gather.2.cloned.1.call-done) | data formatting | bytes 16777216 | tf_op jit(solution)/shard_map/all_gather | solution.py:49
  345.2 6.2 %multiply_reduce_fusion = (f32[2,512]{1,0:T(2,128)S(1)}, bf16[2,512,96]{1,2,0:T(8,128)(2,1)S(1)}, bf16[2,512,96]{1,2,0:T(8,128)(2,1)S(1)}) fusion(f32[2,512,96]{1,2,0:T(8,128)S(1)} %fusion.22, f32[2,512,96]{1,2,0:T(8,128)S(1)} %fusion.23, f32[2,512]{1,0:T(2,128)S(1)} %reshape.150, bf16[2,512,4096]{2,1,0:T(8,128)(2,1)} %bitcast.33, ...), kind=kOutput, calls=%fused_computation.10 | convolution fusion | flops 806976512 | bytes 11149312 | tf_op jit(solution)/shard_map/lrd,lhd->lrh/dot_general | solution.py:58
  351.4 8.3 %fusion.24 = f32[2,512,4096]{2,1,0:T(8,128)} fusion(bf16[2,512,96]{1,2,0:T(8,128)(2,1)S(1)} %get-tuple-element.6, bf16[2,96,4096]{2,1,0:T(8,128)(2,1)S(1)} %copy-done), kind=kOutput, calls=%fused_computation.56 | convolution fusion | flops 805306368 | bytes 18546688 | tf_op jit(solution)/shard_map/lrh,lhd->lrd/dot_general | solution.py:71
  359.8 11.4 %add_convert_fusion = bf16[2,512,4096]{2,1,0:T(8,128)(2,1)} fusion(f32[2,512,4096]{2,1,0:T(8,128)} %fusion.24, bf16[2,512,96]{1,2,0:T(8,128)(2,1)S(1)} %get-tuple-element.7, bf16[2,96,4096]{2,1,0:T(8,128)(2,1)S(1)} %copy-done.4), kind=kOutput, calls=%fused_computation | convolution fusion | flops 813694976 | bytes 26935296 | tf_op jit(solution)/shard_map/lrh,lhd->lrd/dot_general | solution.py:74
  371.2 11.2 %copy.98 = bf16[2,16,32,4096]{3,1,0,2:T(8,128)(2,1)} copy(bf16[2,16,32,4096]{3,2,1,0:T(8,128)(2,1)} %bitcast.35) | data formatting | bytes 16777216 | tf_op jit(solution)/shard_map/convert_element_type | solution.py:88
  382.6 46.2 %psum.7 = f32[2,16,32]{2,1,0:T(8,128)S(1)} all-reduce(f32[2,16,32]{2,1,0:T(8,128)S(1)} %reshape.148), channel_id=1, replica_groups=mesh['expert'=16,'dp'=16] {'dp'}, use_global_device_ids=true, to_apply=%region_5.6 | all-reduce | flops 1024 | bytes 8192 | tf_op jit(solution)/shard_map/psum | solution.py:96
  429.6 5.0 %all-to-all-start.5 = ((f32[2,16,2]{2,0,1:T(2,128)}), f32[2,16,2]{2,0,1:T(2,128)S(1)}, u32[]{:S(2)}, u32[]{:S(2)}) async-start(f32[2,16,2]{2,0,1:T(2,128)} %copy.101), calls=%async_computation.6 | async-start | bytes 32768 | tf_op jit(solution)/shard_map/all_to_all | solution.py:98
  434.6 6.2 %convolution_convert_fusion = bf16[2,96,4096]{2,1,0:T(8,128)(2,1)} fusion(bf16[2,512,4096]{2,1,0:T(8,128)(2,1)} %bitcast.34, f32[2,512]{1,0:T(2,128)S(1)} %reshape.150, f32[2,512,96]{1,2,0:T(8,128)S(1)} %fusion.22, f32[2,512,96]{1,2,0:T(8,128)S(1)} %fusion.23), kind=kOutput, calls=%fused_computation.1 | convolution fusion | flops 806780928 | bytes 10752000 | tf_op jit(solution)/shard_map/lrh,lrd->lhd/dot_general | solution.py:83
  440.8 6.2 %convolution_convert_fusion.2 = bf16[2,96,4096]{2,1,0:T(8,128)(2,1)} fusion(bf16[2,512,96]{1,2,0:T(8,128)(2,1)S(1)} %get-tuple-element.6, bf16[2,512,4096]{2,1,0:T(8,128)(2,1)} %reshape_reshape.3), kind=kOutput, calls=%fused_computation.3 | convolution fusion | flops 806092800 | bytes 10158080 | tf_op jit(solution)/shard_map/lrh,lrd->lhd/dot_general | solution.py:77
  446.9 4.3 reduce-scatter.2.cloned.1.call-done
  451.2 2.4 copy.99
  453.6 7.1 %all-to-all-start.4 = ((bf16[2,16,2,4096]{3,2,0,1:T(2,128)(2,1)}), bf16[2,16,2,4096]{3,2,0,1:T(2,128)(2,1)S(1)}, u32[]{:S(2)}, u32[]{:S(2)}) async-start(bf16[2,16,2,4096]{3,2,0,1:T(2,128)(2,1)} %copy.99), calls=%async_computation.5 | async-start | bytes 1048576 | tf_op jit(solution)/shard_map/all_to_all | solution.py:90
  460.7 6.1 %convolution_convert_fusion.1 = bf16[2,96,4096]{2,1,0:T(8,128)(2,1)} fusion(bf16[2,512,96]{1,2,0:T(8,128)(2,1)S(1)} %get-tuple-element.7, bf16[2,512,4096]{2,1,0:T(8,128)(2,1)} %reshape_reshape.3), kind=kOutput, calls=%fused_computation.2 | convolution fusion | flops 806092800 | bytes 10158080 | tf_op jit(solution)/shard_map/lrh,lrd->lhd/dot_general | solution.py:80
  467.7 1.8 all-to-all-done.4
  (51 shorter events, 8.0 us)
Async XLA Ops:
  7.2 317.7 %copy-start = (bf16[2,96,4096]{2,1,0:T(8,128)(2,1)S(1)}, bf16[2,96,4096]{2,1,0:T(8,128)(2,1)}, u32[]{:S(2)}) copy-start(bf16[2,96,4096]{2,1,0:T(8,128)(2,1)} %param.11) | copy-start | bytes 4718596
  10.2 13.5 %all-to-all-start = ((bf16[2,16,2]{2,0,1:T(2,128)(2,1)}), bf16[2,16,2]{2,0,1:T(2,128)(2,1)S(1)}, u32[]{:S(2)}, u32[]{:S(2)}) async-start(bf16[2,16,2]{2,0,1:T(2,128)(2,1)} %copy.89), calls=%async_computation | async-start | bytes 16384 | tf_op jit(solution)/shard_map/all_to_all | solution.py:43
  23.7 13.9 %all-to-all-start.2 = ((bf16[2,16,2,4096]{3,2,0,1:T(2,128)(2,1)}), bf16[2,16,2,4096]{3,2,0,1:T(2,128)(2,1)S(1)}, u32[]{:S(2)}, u32[]{:S(2)}) async-start(bf16[2,16,2,4096]{3,2,0,1:T(2,128)(2,1)} %copy.95), calls=%async_computation.2 | async-start | bytes 1048576 | tf_op jit(solution)/shard_map/all_to_all | solution.py:37
  37.6 13.6 %all-to-all-start.1 = ((bf16[2,16,2,4096]{3,2,0,1:T(2,128)(2,1)}), bf16[2,16,2,4096]{3,2,0,1:T(2,128)(2,1)S(1)}, u32[]{:S(2)}, u32[]{:S(2)}) async-start(bf16[2,16,2,4096]{3,2,0,1:T(2,128)(2,1)} %copy.92), calls=%async_computation.1 | async-start | bytes 1048576 | tf_op jit(solution)/shard_map/all_to_all | solution.py:40
  59.8 242.5 %all-to-all-start.3 = ((bf16[16,2,16,2,4096]{4,3,2,1,0:T(2,128)(2,1)}), bf16[16,2,16,2,4096]{4,3,2,1,0:T(2,128)(2,1)}, u32[]{:S(2)}, u32[]{:S(2)}) async-start(bf16[16,2,16,2,4096]{4,3,2,1,0:T(2,128)(2,1)} %stack.2), calls=%async_computation.3 | async-start | bytes 16777216 | tf_op jit(solution)/shard_map/all_to_all | solution.py:48
  68.5 265.4 %all-gather.2.cloned.1.call-start = ((), (), s32[]{:S(2)}) async-start(), calls=%async_computation.7 | async-start | bytes 8912896 | tf_op jit(solution)/shard_map/all_gather | solution.py:49
  69.6 381.6 %reduce-scatter.2.cloned.1.call-start = ((), (), s32[]{:S(2)}) async-start(), calls=%async_computation.8 | async-start | bytes 8912896 | tf_op jit(solution)/shard_map/reduce_scatter | solution.py:87
  324.9 6.3 %copy-start.2 = (bf16[2,512,4096]{2,1,0:T(8,128)(2,1)S(1)}, bf16[2,512,4096]{2,1,0:T(8,128)(2,1)}, u32[]{:S(2)}) copy-start(bf16[2,512,4096]{2,1,0:T(8,128)(2,1)} %reshape_reshape.3) | copy-start | bytes 25165828
  324.9 6.3 %copy-start.3 = (bf16[2,96,4096]{2,1,0:T(8,128)(2,1)S(1)}, bf16[2,96,4096]{2,1,0:T(8,128)(2,1)}, u32[]{:S(2)}) copy-start(bf16[2,96,4096]{2,1,0:T(8,128)(2,1)} %param.12) | copy-start | bytes 4718596
  333.9 11.3 %copy-start.5 = (bf16[2,96,4096]{2,1,0:T(8,128)(2,1)S(1)}, bf16[2,96,4096]{2,1,0:T(8,128)(2,1)}, u32[]{:S(2)}) copy-start(bf16[2,96,4096]{2,1,0:T(8,128)(2,1)} %param.13) | copy-start | bytes 4718596
  351.4 8.4 %copy-start.4 = (bf16[2,96,4096]{2,1,0:T(8,128)(2,1)S(1)}, bf16[2,96,4096]{2,1,0:T(8,128)(2,1)}, u32[]{:S(2)}) copy-start(bf16[2,96,4096]{2,1,0:T(8,128)(2,1)} %param.12) | copy-start | bytes 4718596
  429.6 24.1 %all-to-all-start.5 = ((f32[2,16,2]{2,0,1:T(2,128)}), f32[2,16,2]{2,0,1:T(2,128)S(1)}, u32[]{:S(2)}, u32[]{:S(2)}) async-start(f32[2,16,2]{2,0,1:T(2,128)} %copy.101), calls=%async_computation.6 | async-start | bytes 32768 | tf_op jit(solution)/shard_map/all_to_all | solution.py:98
  453.6 15.8 %all-to-all-start.4 = ((bf16[2,16,2,4096]{3,2,0,1:T(2,128)(2,1)}), bf16[2,16,2,4096]{3,2,0,1:T(2,128)(2,1)S(1)}, u32[]{:S(2)}, u32[]{:S(2)}) async-start(bf16[2,16,2,4096]{3,2,0,1:T(2,128)(2,1)} %copy.99), calls=%async_computation.5 | async-start | bytes 1048576 | tf_op jit(solution)/shard_map/all_to_all | solution.py:90
  460.7 10.2 %copy-start.1 = (bf16[2,96,4096]{2,1,0:T(8,128)(2,1)S(1)}, bf16[2,96,4096]{2,1,0:T(8,128)(2,1)}, u32[]{:S(2)}) copy-start(bf16[2,96,4096]{2,1,0:T(8,128)(2,1)} %param.11) | copy-start | bytes 4718596
Sparse Core Ops, SparseCore 0:
  71.7 167.5 all-gather.1
  382.6 68.5 reduce-scatter.1
